TPU v7x, 128 devices: a whole 4x4x4 slice. The times are simulated.
128 devices in a mesh: date: 16 (over z, x), space: 8 (over y, core).
Axes of the slice: x: 4, y: 4, z: 4, core: 2. Of those that a mesh axis runs over, the one named last changes fastest.
Arguments:
- frames: bfloat16 [64, 2048, 1024], P('date', 'space'), may hold values from -6 to 6
- cloud_mask: int32 [64, 2048], P('date', 'space'), may hold values from 0 to 1
- qkv_weight: bfloat16 [2, 1024, 3072], replicated, may hold values from -0.1875 to 0.1875
- out_weight: bfloat16 [2, 1024, 1024], replicated, may hold values from -0.1875 to 0.1875
- norm_gain: float32 [2, 1024], replicated, may hold values from 0.1 to 1.9
- head_norm_scale: float32 [2, 1024], replicated, may hold values from 0.1 to 1.9
- decay: float32 [2, 64, 16], P(None, 'date'), as said below
Outputs:
- forecast: bfloat16 [64, 2048, 1024], P('date', 'space')
Inputs may be any that keep to these rules, and one draw needn't show every extreme that they name: `decay`: every entry lies strictly between 0 and 1.
All inputs are finite; a program needn't handle non-finite values.
Results may differ from a plain program's by a relative error of at most 0.0065.
Values may be sent and summed in bfloat16 or wider, within the bound.
No kernel may reach another device: no remote copies, remote signals or barrier semaphores. Data moves between devices by JAX's collectives and lax.ppermute only.
A program may use at most 128 MiB of HBM per device.

v0:
```python
import jax
import jax.numpy as jnp
from jax import lax
from jax.sharding import PartitionSpec as P

HEADS = 16
HEAD = 64
STACK_LEVELS = 2


def carried_in(value, axis, join, neutral):
    count, mine = (lax.axis_size(axis), lax.axis_index(axis))
    pieces = jax.tree.map(lambda part: lax.all_gather(part, axis), value)
    subtotal = jax.tree.map(
        lambda part, zero: jnp.full_like(part, 0) + jnp.asarray(zero, part.dtype), value, neutral
    )

    def step(position, subtotal):
        longer = join(subtotal, jax.tree.map(lambda part: part[position], pieces))
        return jax.tree.map(lambda new, old: jnp.where(position < mine, new, old), longer, subtotal)

    return lax.fori_loop(0, count - 1, step, subtotal)


def feature(u):
    return jax.nn.elu(u) + 1.0


def chain(earlier, later):
    return (earlier[0] * later[1][:, None, None] + later[0], earlier[1] * later[1])


def shards(frames, cloud_mask, qkv_weight, out_weight, norm_gain, head_norm_scale, decay):
    dates_here, tokens_here, width = frames.shape
    heads = HEADS
    current = frames
    flag_f = cloud_mask.astype(jnp.float32)[:, :, None]
    for layer in range(STACK_LEVELS):
        xf = current.astype(jnp.float32)
        in_msq = jnp.mean(xf * xf, -1, keepdims=True) + 1e-05
        normalized_output = (xf * lax.rsqrt(in_msq) * norm_gain[layer]).astype(jnp.bfloat16)
        proj = jnp.dot(
            normalized_output.reshape(-1, width),
            qkv_weight[layer],
            preferred_element_type=jnp.float32,
        )
        proj = proj.reshape(dates_here, tokens_here, 3 * width)
        query = (
            feature(proj[:, :, :width])
            .astype(jnp.bfloat16)
            .reshape(dates_here, tokens_here, heads, HEAD)
        )
        key = (
            (feature(proj[:, :, width : 2 * width]) * flag_f)
            .astype(jnp.bfloat16)
            .reshape(dates_here, tokens_here, heads, HEAD)
        )
        value = (
            proj[:, :, 2 * width :]
            .astype(jnp.bfloat16)
            .reshape(dates_here, tokens_here, heads, HEAD)
        )
        pairing_partial = jnp.einsum(
            "tshe,tshf->thef", key, value, preferred_element_type=jnp.float32
        )
        kv = lax.psum(pairing_partial, "space")
        persist_factor = decay[layer]

        def advance(state, inputs):
            state = inputs[1][:, None, None] * state + inputs[0]
            return (state, state)

        start = jnp.zeros((heads, HEAD, HEAD), jnp.float32)
        last_state, local_states = lax.scan(advance, start, (kv, persist_factor))
        kept = jnp.cumprod(persist_factor, axis=0)
        total_kept = kept[-1]
        incoming, _ = carried_in(
            (last_state, total_kept),
            "date",
            chain,
            (jnp.zeros_like(last_state), jnp.ones_like(total_kept)),
        )
        states = local_states + kept[:, :, None, None] * incoming[None]
        state_b = states.astype(jnp.bfloat16)
        numer = jnp.einsum("tshe,thef->tshf", query, state_b, preferred_element_type=jnp.float32)
        head_msq = jnp.mean(numer * numer, -1, keepdims=True) + 1e-05
        numer = numer * lax.rsqrt(head_msq)
        mixed = (numer.reshape(dates_here, tokens_here, width) * head_norm_scale[layer]).astype(
            jnp.bfloat16
        )
        update = jnp.dot(
            mixed.reshape(-1, width), out_weight[layer], preferred_element_type=jnp.float32
        )
        current = (xf + update.reshape(dates_here, tokens_here, width)).astype(jnp.bfloat16)
    return current


def solution(mesh):
    placed = (
        P("date", "space", None),
        P("date", "space"),
        P(),
        P(),
        P(),
        P(),
        P(None, "date", None),
    )
    return jax.shard_map(
        shards, mesh=mesh, in_specs=placed, out_specs=P("date", "space", None), check_vma=False
    )
```

profile of v0, /device:TPU:1, one launch (start us, length us, event | category | flops | bytes accessed | tf_op | source)
XLA Modules:
  0.0 406.9 jit_solution(10266856537543714752)
XLA Ops:
  7.4 2.1 fusion.10
  9.5 8.9 %fusion.6 = f32[4,256,3072]{2,1,0:T(8,128)S(1)} fusion(bf16[2,1024,3072]{2,1,0:T(8,128)(2,1)} %param.17, bf16[4,256,1024]{2,1,0:T(8,128)(2,1)S(1)} %copy-done.4, f32[1024]{0:T(1024)S(1)} %bitcast.125, f32[4,256]{1,0:T(4,128)S(1)} %add_rsqrt_fusion.3), kind=kOutput, calls=%fused_computation.26 | convolution fusion | flops 6446645248 | bytes 20979712 | tf_op jit(solution)/shard_map/dot_general | solution.py:42
  18.4 1.7 slice.113
  20.1 5.1 %fusion.21 = (bf16[4,256,1024]{2,1,0:T(8,128)(2,1)}, bf16[4,256,1024]{2,1,0:T(8,128)(2,1)}) fusion(f32[4,256,3072]{2,1,0:T(8,128)S(1)} %fusion.6, f32[4,256]{1,0:T(4,128)S(1)} %convert_element_type.59), kind=kLoop, calls=%fused_computation.47 | loop fusion | flops 11534336 | bytes 12587008 | tf_op jit(solution)/shard_map/convert_element_type | solution.py:55
  25.2 2.8 copy.28
  28.0 3.9 copy.29
  32.0 3.6 fusion.61
  36.3 66.5 %all-reduce.3.cloned.1.call-done = f32[4,16,64,64]{3,2,1,0:T(8,128)} async-done(((f32[4,16,64,64]{3,2,1,0:T(8,128)}), f32[4,16,64,64]{3,2,1,0:T(8,128)}) %all-reduce.3.cloned.1.call-update) | async-done | bytes 1048592 | tf_op jit(solution)/shard_map/psum | solution.py:66
  103.0 4.9 %while.54 = (s32[]{:T(128)}, f32[16,64,64]{2,1,0:T(8,128)S(1)}, f32[4,16,64,64]{3,2,1,0:T(8,128)S(1)}, f32[4,16]{1,0:T(4,128)S(1)}, f32[4,16,64,64]{3,2,1,0:T(8,128)}, /*index=5*/s32[]{:T(128)}, s32[]{:T(128)}) while((s32[]{:T(128)}, f32[16,64,64]{2,1,0:T(8,128)S(1)}, f32[4,16,64,64]{3,2,1,0:T(8,128)S(1)}, f32[4,16]{1,0:T(4,128)S(1)}, ...), condition=%wide.region_3.4_spmd.clone, body=%wide.region_2.3_spmd.clone.sunk | while | flops 196611 | bytes 1835743 | solution.py:74
  103.0 1.2 bitcast_dynamic-update-slice_fusion.4
  104.2 1.2 bitcast_dynamic-update-slice_fusion.4
  105.4 1.2 bitcast_dynamic-update-slice_fusion.4
  106.7 1.2 bitcast_dynamic-update-slice_fusion.4
  109.4 2.9 copy.30
  112.3 17.2 %all-gather.2 = f32[16,1,16]{2,1,0:T(1,128)S(1)} all-gather(f32[1,1,16]{2,1,0:T(1,128)S(1)} %slice_bitcast_fusion.3), channel_id=1, replica_groups=mesh['date'=16,'space'=8] {'date'}, dimensions={0}, use_global_device_ids=true | all-gather | bytes 1088 | tf_op jit(solution)/shard_map/all_gather | solution.py:13
  129.6 51.7 %all-gather.7.cloned.1.call-done = f32[256,64,64]{2,1,0:T(8,128)} async-done(((f32[16,64,64]{2,1,0:T(8,128)}), f32[256,64,64]{2,1,0:T(8,128)}) %all-gather.7.cloned.1.call-update) | async-done | bytes 4194320 | tf_op jit(solution)/shard_map/all_gather | solution.py:13
  181.2 18.2 %while.55 = (s32[]{:T(128)}, f32[16,64,64]{2,1,0:T(8,128)S(1)}, s32[]{:T(128)}, f32[16,16]{1,0:T(8,128)S(1)}, f32[16,16,64,64]{3,2,1,0:T(8,128)}, /*index=5*/s32[]{:T(128)}, s32[]{:T(128)}) while((s32[]{:T(128)}, f32[16,64,64]{2,1,0:T(8,128)S(1)}, s32[]{:T(128)}, f32[16,16]{1,0:T(8,128)S(1)}, f32[16,16,64,64]{3,2,1,0:T(8,128)}, ...), condition=%wide.region_6.7_spmd.clone, body=%wide.region_5.6_spmd.clone.sunk | while | flops 262148 | bytes 786729 | solution.py:22
  184.9 1.2 fusion.76
  186.1 1.2 fusion.76
  187.3 1.2 fusion.76
  190.9 1.2 fusion.76
  192.1 1.2 fusion.76
  195.8 1.2 fusion.76
  197.0 1.2 fusion.76
  198.2 1.2 fusion.76
  199.4 2.7 fusion.35
  202.7 1.3 copy-done.5
  204.1 2.7 fusion.14
  206.8 6.8 %fusion.4 = f32[4,256,3072]{2,1,0:T(8,128)S(1)} fusion(bf16[2,1024,3072]{2,1,0:T(8,128)(2,1)S(1)} %bitcast.127, bf16[4,256,1024]{2,1,0:T(8,128)(2,1)S(1)} %get-tuple-element.384, f32[1024]{0:T(1024)S(1)} %bitcast.124, f32[4,256]{1,0:T(4,128)S(1)} %add_rsqrt_fusion.2), kind=kOutput, calls=%fused_computation.24 | convolution fusion | flops 6446645248 | bytes 20979712 | tf_op jit(solution)/shard_map/dot_general | solution.py:42
  213.6 5.1 %fusion.28 = (bf16[4,256,1024]{2,1,0:T(8,128)(2,1)}, bf16[4,256,1024]{2,1,0:T(8,128)(2,1)}) fusion(f32[4,256,3072]{2,1,0:T(8,128)S(1)} %fusion.4, f32[4,256]{1,0:T(4,128)S(1)} %convert_element_type.59), kind=kLoop, calls=%fused_computation.54 | loop fusion | flops 11534336 | bytes 12587008 | tf_op jit(solution)/shard_map/convert_element_type | solution.py:55
  218.7 1.6 slice.112
  220.4 2.8 copy.33
  223.2 3.9 copy.34
  227.2 3.6 fusion.62
  231.1 63.4 %all-reduce.5.cloned.1.call-done = f32[4,16,64,64]{3,2,1,0:T(8,128)} async-done(((f32[4,16,64,64]{3,2,1,0:T(8,128)}), f32[4,16,64,64]{3,2,1,0:T(8,128)}) %all-reduce.5.cloned.1.call-update) | async-done | bytes 1048592 | tf_op jit(solution)/shard_map/psum | solution.py:66
  294.7 4.9 %while.56 = (s32[]{:T(128)}, f32[16,64,64]{2,1,0:T(8,128)S(1)}, f32[4,16,64,64]{3,2,1,0:T(8,128)S(1)}, f32[4,16]{1,0:T(4,128)S(1)}, f32[4,16,64,64]{3,2,1,0:T(8,128)}, /*index=5*/s32[]{:T(128)}, s32[]{:T(128)}) while((s32[]{:T(128)}, f32[16,64,64]{2,1,0:T(8,128)S(1)}, f32[4,16,64,64]{3,2,1,0:T(8,128)S(1)}, ...), condition=%wide.region_11.12_spmd.clone, body=%wide.region_10.11_spmd.clone.sunk | while | flops 196611 | bytes 1835743 | solution.py:74
  294.7 1.2 bitcast_dynamic-update-slice_fusion.5
  296.0 1.2 bitcast_dynamic-update-slice_fusion.5
  297.2 1.2 bitcast_dynamic-update-slice_fusion.5
  298.4 1.2 bitcast_dynamic-update-slice_fusion.5
  300.6 16.6 %all-gather.3 = f32[16,1,16]{2,1,0:T(1,128)S(1)} all-gather(f32[1,1,16]{2,1,0:T(1,128)S(1)} %slice_bitcast_fusion.2), channel_id=1, replica_groups=mesh['date'=16,'space'=8] {'date'}, dimensions={0}, use_global_device_ids=true | all-gather | bytes 1088 | tf_op jit(solution)/shard_map/all_gather | solution.py:13
  317.2 2.9 copy.35
  320.1 52.9 %all-gather.9.cloned.1.call-done = f32[256,64,64]{2,1,0:T(8,128)} async-done(((f32[16,64,64]{2,1,0:T(8,128)}), f32[256,64,64]{2,1,0:T(8,128)}) %all-gather.9.cloned.1.call-update) | async-done | bytes 4194320 | tf_op jit(solution)/shard_map/all_gather | solution.py:13
  373.0 18.2 %while.57 = (s32[]{:T(128)}, f32[16,64,64]{2,1,0:T(8,128)S(1)}, s32[]{:T(128)}, f32[16,16]{1,0:T(8,128)S(1)}, f32[16,16,64,64]{3,2,1,0:T(8,128)}, /*index=5*/s32[]{:T(128)}, s32[]{:T(128)}) while((s32[]{:T(128)}, f32[16,64,64]{2,1,0:T(8,128)S(1)}, s32[]{:T(128)}, f32[16,16]{1,0:T(8,128)S(1)}, f32[16,16,64,64]{3,2,1,0:T(8,128)}, ...), condition=%wide.region_14.15_spmd.clone, body=%wide.region_13.14_spmd.clone.sunk | while | flops 262148 | bytes 786729 | solution.py:22
  374.2 1.2 fusion.78
  391.1 2.6 fusion.32
  394.3 1.6 copy-done.10
  396.6 3.7 fusion.17
  (120 shorter events, 31.6 us)
Async XLA Ops:
  6.5 3.0 copy-start.4
  6.5 3.0 copy-start.7
  6.5 96.2 %all-reduce.3.cloned.1.call-start = ((), (), s32[]{:S(2)}) async-start(), calls=%async_computation | async-start | bytes 4194304 | tf_op jit(solution)/shard_map/psum | solution.py:66
  35.6 0.7 copy-start.8
  35.6 145.6 %all-gather.7.cloned.1.call-start = ((), (), s32[]{:S(2)}) async-start(), calls=%async_computation.2 | async-start | bytes 8912896 | tf_op jit(solution)/shard_map/all_gather | solution.py:13
  107.9 0.8 copy-start
  107.9 1.5 copy-start.3
  108.7 185.8 %all-reduce.5.cloned.1.call-start = ((), (), s32[]{:S(2)}) async-start(), calls=%async_computation.1 | async-start | bytes 4194304 | tf_op jit(solution)/shard_map/psum | solution.py:66
  109.4 2.9 copy-start.6
  199.4 3.3 copy-start.9
  199.4 7.4 %slice-start = ((s8[12582912]{0:T(1024)(128)(4,1)}), s8[4194304]{0:T(1024)(128)(4,1)S(1)}, s32[]{:S(2)}) async-start(s8[12582912]{0:T(1024)(128)(4,1)} %bitcast.126), calls=%async_computation.4 | async-start | bytes 8388608
  202.2 1.9 copy-start.5
  202.2 4.6 %slice-start.1 = ((s8[12582912]{0:T(1024)(128)(4,1)}), s8[4194304]{0:T(1024)(128)(4,1)S(1)}, s32[]{:S(2)}) async-start(s8[12582912]{0:T(1024)(128)(4,1)} %bitcast.126), calls=%async_computation.5 | async-start | bytes 8388608
  204.1 2.8 slice-start.2
  206.8 6.8 %copy-start.11 = (bf16[4,256,1024]{2,1,0:T(8,128)(2,1)}, bf16[4,256,1024]{2,1,0:T(8,128)(2,1)S(1)}, u32[]{:S(2)}) copy-start(bf16[4,256,1024]{2,1,0:T(8,128)(2,1)S(1)} %get-tuple-element.384) | copy-start | bytes 6291460
  230.8 142.2 %all-gather.9.cloned.1.call-start = ((), (), s32[]{:S(2)}) async-start(), calls=%async_computation.3 | async-start | bytes 8912896 | tf_op jit(solution)/shard_map/all_gather | solution.py:13
  299.6 0.8 copy-start.1
  299.6 17.6 %copy-start.2 = (f32[4,16,64,64]{3,2,1,0:T(8,128)}, f32[4,16,64,64]{3,2,1,0:T(8,128)S(1)}, u32[]{:S(2)}) copy-start(f32[4,16,64,64]{3,2,1,0:T(8,128)S(1)} %get-tuple-element.252) | copy-start | bytes 3145732
  393.7 2.2 copy-start.10
  393.8 2.9 copy-start.12
Sparse Core Ops, SparseCore 0:
  35.7 66.9 all-reduce.2
  108.8 72.3 all-gather.6
  230.9 63.4 all-reduce.4
  300.6 72.3 all-gather.8
where the time goes:
time: 409 us; the launch traced here: 407 us
  waiting for transfers between devices  234 us (57%)
  other arithmetic  58.1 us (14%)
  matrix products  34.5 us (8%)
  blocking collectives  33.8 us (8%)
  local copies, waits for them, and re-layouts  30.9 us (8%)
  between operations  13.5 us (3%)
    psum x2, waiting for transfers between devices, shards(): kv = lax.psum(pairing_partial, 'space')  130 us
    all_gather x2, waiting for transfers between devices, carried_in(): pieces = jax.tree.map(lambda part: lax.all_gather(part, axis), value)  105 us
    select_n x30, other arithmetic, step(): jnp.where(position < mine, new, old)  35.2 us
    all_gather x2, blocking collectives, carried_in(): pieces = jax.tree.map(lambda part: lax.all_gather(part, axis), value)  33.8 us
    dot_general x2, matrix products, shards(): jnp.dot(normalized_output.reshape(-1, width), qkv_weight[layer], preferre...  15.6 us
    slice x4, local copies, waits for them, and re-layouts, shards(): proj[:, :, 2 * width:].astype(jnp.bfloat16)  11.2 us
    convert_element_type x2, other arithmetic, shards(): key = (feature(proj[:, :, width:2 * width]) * flag_f).astype(jnp.bfloat16...  10.2 us
    dynamic_update_slice x8, other arithmetic, shards(): last_state, local_states = lax.scan(advance, start, (kv, persist_factor))  9.48 us
  transfers between devices with their start and end apart: 4, of which 4 were waited for; matrix products, arithmetic and copies ran while one was open for 1% of the time, Pallas kernels for 0%

commit v1 on v0

--- a/solution.py
+++ b/solution.py
@@ -63,7 +63,9 @@
         pairing_partial = jnp.einsum(
             "tshe,tshf->thef", key, value, preferred_element_type=jnp.float32
         )
-        kv = lax.psum(pairing_partial, "space")
+        kv = pairing_partial
+        for hop in (1, 2, 4):
+            kv = kv + lax.ppermute(kv, "space", [(dev, dev ^ hop) for dev in range(8)])
         persist_factor = decay[layer]
 
         def advance(state, inputs):

time: 409 us -> 485 us (1.19)
  waiting for transfers between devices: 234 us -> 294 us
  starting transfers between devices: 0.35 us -> 11.4 us
  other arithmetic: 58.1 us -> 63.3 us
    ppermute x0 -> x6, waiting for transfers between devices: none -> 188 us  [shards(): kv = kv + lax.ppermute(kv, 'space', [(dev, dev ^ hop) for dev in range(8)])]
    psum x2 -> x0, waiting for transfers between devices: 130 us -> none  [shards(): kv = lax.psum(pairing_partial, 'space')]
    ppermute x0 -> x6, starting transfers between devices: none -> 11.3 us  [shards(): kv = kv + lax.ppermute(kv, 'space', [(dev, dev ^ hop) for dev in range(8)])]
    add x0 -> x6, other arithmetic: none -> 7.11 us  [shards(): kv = kv + lax.ppermute(kv, 'space', [(dev, dev ^ hop) for dev in range(8)])]
  transfers between devices with their start and end apart: 4 -> 8, of which waited for: 4 -> 8; matrix products, arithmetic and copies ran while one was open for 1% -> 1% of each run, Pallas kernels for 0% -> 0%
where the time goes in v1:
time: 485 us; the launch traced here: 483 us
  waiting for transfers between devices  294 us (61%)
  other arithmetic  63.3 us (13%)
  blocking collectives  34.6 us (7%)
  local copies, waits for them, and re-layouts  32.5 us (7%)
  matrix products  31.9 us (7%)
  between operations  13.8 us (3%)
  starting transfers between devices  11.4 us (2%)
    ppermute x6, waiting for transfers between devices, shards(): kv = kv + lax.ppermute(kv, 'space', [(dev, dev ^ hop) for dev in range(8)])  188 us
    all_gather x2, waiting for transfers between devices, carried_in(): pieces = jax.tree.map(lambda part: lax.all_gather(part, axis), value)  106 us
    select_n x30, other arithmetic, step(): jnp.where(position < mine, new, old)  35.2 us
    all_gather x2, blocking collectives, carried_in(): pieces = jax.tree.map(lambda part: lax.all_gather(part, axis), value)  34.6 us
    dot_general x2, matrix products, shards(): jnp.dot(normalized_output.reshape(-1, width), qkv_weight[layer], preferre...  15.6 us
    ppermute x6, starting transfers between devices, shards(): kv = kv + lax.ppermute(kv, 'space', [(dev, dev ^ hop) for dev in range(8)])  11.3 us
    slice x4, local copies, waits for them, and re-layouts, shards(): proj[:, :, 2 * width:].astype(jnp.bfloat16)  11.2 us
    convert_element_type x2, other arithmetic, shards(): key = (feature(proj[:, :, width:2 * width]) * flag_f).astype(jnp.bfloat16...  10.3 us
  transfers between devices with their start and end apart: 8, of which 8 were waited for; matrix products, arithmetic and copies ran while one was open for 1% of the time, Pallas kernels for 0%

profile of v1, /device:TPU:1, one launch (start us, length us, event | category | flops | bytes accessed | tf_op | source)
XLA Modules:
  0.0 482.5 jit_solution(2082037682731890510)
XLA Ops:
  7.4 2.1 fusion.10
  9.5 8.9 %fusion.6 = f32[4,256,3072]{2,1,0:T(8,128)S(1)} fusion(bf16[2,1024,3072]{2,1,0:T(8,128)(2,1)} %param.17, bf16[4,256,1024]{2,1,0:T(8,128)(2,1)S(1)} %copy-done.4, f32[1024]{0:T(1024)S(1)} %bitcast.125, f32[4,256]{1,0:T(4,128)S(1)} %add_rsqrt_fusion.3), kind=kOutput, calls=%fused_computation.26 | convolution fusion | flops 6446645248 | bytes 20979712 | tf_op jit(solution)/shard_map/dot_general | solution.py:42
  18.4 1.7 slice.113
  20.1 5.1 %fusion.21 = (bf16[4,256,1024]{2,1,0:T(8,128)(2,1)}, bf16[4,256,1024]{2,1,0:T(8,128)(2,1)}) fusion(f32[4,256,3072]{2,1,0:T(8,128)S(1)} %fusion.6, f32[4,256]{1,0:T(4,128)S(1)} %convert_element_type.59), kind=kLoop, calls=%fused_computation.47 | loop fusion | flops 11534336 | bytes 12587008 | tf_op jit(solution)/shard_map/convert_element_type | solution.py:55
  25.2 2.8 copy.28
  28.1 3.9 copy.29
  32.0 2.3 fusion.61
  34.3 1.5 collective-permute-start
  35.8 3.8 collective-permute-done
  40.1 1.5 collective-permute-start.1
  41.6 45.4 %collective-permute-done.1 = f32[4,16,64,64]{3,2,1,0:T(8,128)S(1)} collective-permute-done((f32[4,16,64,64]{3,2,1,0:T(8,128)S(1)}, f32[4,16,64,64]{3,2,1,0:T(8,128)S(1)}, u32[]{:S(2)}, u32[]{:S(2)}) %collective-permute-start.1) | collective-permute-done | bytes 1048608 | tf_op jit(solution)/shard_map/ppermute | solution.py:68
  87.4 3.1 collective-permute-start.2
  90.5 44.7 %collective-permute-done.2 = f32[4,16,64,64]{3,2,1,0:T(8,128)} collective-permute-done((f32[4,16,64,64]{3,2,1,0:T(8,128)S(1)}, f32[4,16,64,64]{3,2,1,0:T(8,128)}, u32[]{:S(2)}, u32[]{:S(2)}) %collective-permute-start.2) | collective-permute-done | bytes 1048608 | tf_op jit(solution)/shard_map/ppermute | solution.py:68
  135.2 2.6 add.148
  137.8 1.6 broadcast.94.clone
  139.4 3.8 while.54
  144.1 2.9 copy.30
  147.1 18.5 %all-gather.2 = f32[16,1,16]{2,1,0:T(1,128)S(1)} all-gather(f32[1,1,16]{2,1,0:T(1,128)S(1)} %slice_bitcast_fusion.3), channel_id=1, replica_groups=mesh['date'=16,'space'=8] {'date'}, dimensions={0}, use_global_device_ids=true | all-gather | bytes 1088 | tf_op jit(solution)/shard_map/all_gather | solution.py:13
  165.6 53.2 %all-gather.7.cloned.1.call-done = f32[256,64,64]{2,1,0:T(8,128)} async-done(((f32[16,64,64]{2,1,0:T(8,128)}), f32[256,64,64]{2,1,0:T(8,128)}) %all-gather.7.cloned.1.call-update) | async-done | bytes 4194320 | tf_op jit(solution)/shard_map/all_gather | solution.py:13
  218.8 18.2 %while.55 = (s32[]{:T(128)}, f32[16,64,64]{2,1,0:T(8,128)S(1)}, s32[]{:T(128)}, f32[16,16]{1,0:T(8,128)S(1)}, f32[16,16,64,64]{3,2,1,0:T(8,128)}, /*index=5*/s32[]{:T(128)}, s32[]{:T(128)}) while((s32[]{:T(128)}, f32[16,64,64]{2,1,0:T(8,128)S(1)}, s32[]{:T(128)}, f32[16,16]{1,0:T(8,128)S(1)}, f32[16,16,64,64]{3,2,1,0:T(8,128)}, ...), condition=%wide.region_5.6_spmd.clone, body=%wide.region_4.5_spmd.clone.sunk | while | flops 262148 | bytes 786729 | solution.py:22
  220.0 1.2 fusion.76
  223.6 1.2 fusion.76
  224.8 1.2 fusion.76
  226.1 1.2 fusion.76
  237.0 2.7 fusion.35
  240.3 1.3 copy-done.5
  241.6 2.7 fusion.14
  244.4 6.8 %fusion.4 = f32[4,256,3072]{2,1,0:T(8,128)S(1)} fusion(bf16[2,1024,3072]{2,1,0:T(8,128)(2,1)S(1)} %bitcast.127, bf16[4,256,1024]{2,1,0:T(8,128)(2,1)S(1)} %get-tuple-element.384, f32[1024]{0:T(1024)S(1)} %bitcast.124, f32[4,256]{1,0:T(4,128)S(1)} %add_rsqrt_fusion.2), kind=kOutput, calls=%fused_computation.24 | convolution fusion | flops 6446645248 | bytes 20979712 | tf_op jit(solution)/shard_map/dot_general | solution.py:42
  251.2 5.1 %fusion.28 = (bf16[4,256,1024]{2,1,0:T(8,128)(2,1)}, bf16[4,256,1024]{2,1,0:T(8,128)(2,1)}) fusion(f32[4,256,3072]{2,1,0:T(8,128)S(1)} %fusion.4, f32[4,256]{1,0:T(4,128)S(1)} %convert_element_type.59), kind=kLoop, calls=%fused_computation.54 | loop fusion | flops 11534336 | bytes 12587008 | tf_op jit(solution)/shard_map/convert_element_type | solution.py:55
  256.3 1.6 slice.112
  257.9 2.8 copy.33
  260.8 3.9 copy.34
  264.7 2.3 fusion.62
  268.1 3.8 collective-permute-done.3
  272.5 1.3 collective-permute-start.4
  273.8 45.6 %collective-permute-done.4 = f32[4,16,64,64]{3,2,1,0:T(8,128)S(1)} collective-permute-done((f32[4,16,64,64]{3,2,1,0:T(8,128)S(1)}, f32[4,16,64,64]{3,2,1,0:T(8,128)S(1)}, u32[]{:S(2)}, u32[]{:S(2)}) %collective-permute-start.4) | collective-permute-done | bytes 1048608 | tf_op jit(solution)/shard_map/ppermute | solution.py:68
  319.8 2.8 collective-permute-start.5
  322.6 44.8 %collective-permute-done.5 = f32[4,16,64,64]{3,2,1,0:T(8,128)} collective-permute-done((f32[4,16,64,64]{3,2,1,0:T(8,128)S(1)}, f32[4,16,64,64]{3,2,1,0:T(8,128)}, u32[]{:S(2)}, u32[]{:S(2)}) %collective-permute-start.5) | collective-permute-done | bytes 1048608 | tf_op jit(solution)/shard_map/ppermute | solution.py:68
  367.4 2.6 add.157
  370.1 1.6 broadcast.94
  371.6 3.8 while.56
  376.4 16.1 %all-gather.3 = f32[16,1,16]{2,1,0:T(1,128)S(1)} all-gather(f32[1,1,16]{2,1,0:T(1,128)S(1)} %slice_bitcast_fusion.2), channel_id=1, replica_groups=mesh['date'=16,'space'=8] {'date'}, dimensions={0}, use_global_device_ids=true | all-gather | bytes 1088 | tf_op jit(solution)/shard_map/all_gather | solution.py:13
  392.5 2.9 copy.35
  395.3 53.0 %all-gather.9.cloned.1.call-done = f32[256,64,64]{2,1,0:T(8,128)} async-done(((f32[16,64,64]{2,1,0:T(8,128)}), f32[256,64,64]{2,1,0:T(8,128)}) %all-gather.9.cloned.1.call-update) | async-done | bytes 4194320 | tf_op jit(solution)/shard_map/all_gather | solution.py:13
  448.3 18.2 %while.57 = (s32[]{:T(128)}, f32[16,64,64]{2,1,0:T(8,128)S(1)}, s32[]{:T(128)}, f32[16,16]{1,0:T(8,128)S(1)}, f32[16,16,64,64]{3,2,1,0:T(8,128)}, /*index=5*/s32[]{:T(128)}, s32[]{:T(128)}) while((s32[]{:T(128)}, f32[16,64,64]{2,1,0:T(8,128)S(1)}, s32[]{:T(128)}, f32[16,16]{1,0:T(8,128)S(1)}, f32[16,16,64,64]{3,2,1,0:T(8,128)}, ...), condition=%wide.region_12.13_spmd.clone, body=%wide.region_11.12_spmd.clone.sunk | while | flops 262148 | bytes 786729 | solution.py:22
  466.5 2.6 fusion.32
  469.6 1.6 copy-done.10
  472.0 3.7 fusion.17
  (132 shorter events, 46.0 us)
Async XLA Ops:
  6.5 3.0 copy-start.4
  6.5 3.0 copy-start.7
  6.5 212.2 %all-gather.7.cloned.1.call-start = ((), (), s32[]{:S(2)}) async-start(), calls=%async_computation | async-start | bytes 8912896 | tf_op jit(solution)/shard_map/all_gather | solution.py:13
  34.3 5.2 %collective-permute-start = (f32[4,16,64,64]{3,2,1,0:T(8,128)S(1)}, f32[4,16,64,64]{3,2,1,0:T(8,128)S(1)}, u32[]{:S(2)}, u32[]{:S(2)}) collective-permute-start(f32[4,16,64,64]{3,2,1,0:T(8,128)S(1)} %fusion.61), channel_id=1, source_target_pairs={{0,1},{1,0},{2,3},{3,2},{4,5},{5,4},{6,7},{7,6},{8,9},{9,8},{10,11... | collective-permute-start | bytes 3145736 | tf_op jit(solution)/shard_map/ppermute | solution.py:68
  40.1 50.4 %copy-start.8 = (f32[2,4,16]{2,1,0:T(4,128)S(1)}, f32[2,4,16]{2,1,0:T(4,128)}, u32[]{:S(2)}) copy-start(f32[2,4,16]{2,1,0:T(4,128)} %param.21) | copy-start | bytes 1540
  40.1 46.9 %collective-permute-start.1 = (f32[4,16,64,64]{3,2,1,0:T(8,128)S(1)}, f32[4,16,64,64]{3,2,1,0:T(8,128)S(1)}, u32[]{:S(2)}, u32[]{:S(2)}) collective-permute-start(f32[4,16,64,64]{3,2,1,0:T(8,128)S(1)} %add.146), channel_id=1, source_target_pairs={{0,2},{1,3},{2,0},{3,1},{4,6},{5,7},{6,4},{7,5},{8,10},{9,11},{10,... | collective-permute-start | bytes 3145736 | tf_op jit(solution)/shard_map/ppermute | solution.py:68
  87.4 3.1 copy-start.2
  87.4 47.8 %collective-permute-start.2 = (f32[4,16,64,64]{3,2,1,0:T(8,128)S(1)}, f32[4,16,64,64]{3,2,1,0:T(8,128)}, u32[]{:S(2)}, u32[]{:S(2)}) collective-permute-start(f32[4,16,64,64]{3,2,1,0:T(8,128)S(1)} %add.147), channel_id=1, source_target_pairs={{0,4},{1,5},{2,6},{3,7},{4,0},{5,1},{6,2},{7,3},{8,12},{9,13},{10,... | collective-permute-start | bytes 3145736 | tf_op jit(solution)/shard_map/ppermute | solution.py:68
  143.1 0.8 copy-start
  144.0 304.3 %all-gather.9.cloned.1.call-start = ((), (), s32[]{:S(2)}) async-start(), calls=%async_computation.1 | async-start | bytes 8912896 | tf_op jit(solution)/shard_map/all_gather | solution.py:13
  144.1 2.9 copy-start.6
  237.0 3.3 copy-start.9
  237.0 7.4 %slice-start = ((s8[12582912]{0:T(1024)(128)(4,1)}), s8[4194304]{0:T(1024)(128)(4,1)S(1)}, s32[]{:S(2)}) async-start(s8[12582912]{0:T(1024)(128)(4,1)} %bitcast.126), calls=%async_computation.2 | async-start | bytes 8388608
  239.7 1.9 copy-start.5
  239.8 4.6 slice-start.1
  241.6 2.8 slice-start.2
  244.3 6.8 %copy-start.11 = (bf16[4,256,1024]{2,1,0:T(8,128)(2,1)}, bf16[4,256,1024]{2,1,0:T(8,128)(2,1)S(1)}, u32[]{:S(2)}) copy-start(bf16[4,256,1024]{2,1,0:T(8,128)(2,1)S(1)} %get-tuple-element.384) | copy-start | bytes 6291460
  267.0 4.9 %collective-permute-start.3 = (f32[4,16,64,64]{3,2,1,0:T(8,128)S(1)}, f32[4,16,64,64]{3,2,1,0:T(8,128)S(1)}, u32[]{:S(2)}, u32[]{:S(2)}) collective-permute-start(f32[4,16,64,64]{3,2,1,0:T(8,128)S(1)} %fusion.62), channel_id=1, source_target_pairs={{0,1},{1,0},{2,3},{3,2},{4,5},{5,4},{6,7},{7,6},{8,9},{9,8},{10,11... | collective-permute-start | bytes 3145736 | tf_op jit(solution)/shard_map/ppermute | solution.py:68
  272.5 46.9 %collective-permute-start.4 = (f32[4,16,64,64]{3,2,1,0:T(8,128)S(1)}, f32[4,16,64,64]{3,2,1,0:T(8,128)S(1)}, u32[]{:S(2)}, u32[]{:S(2)}) collective-permute-start(f32[4,16,64,64]{3,2,1,0:T(8,128)S(1)} %add.155), channel_id=1, source_target_pairs={{0,2},{1,3},{2,0},{3,1},{4,6},{5,7},{6,4},{7,5},{8,10},{9,11},{10,... | collective-permute-start | bytes 3145736 | tf_op jit(solution)/shard_map/ppermute | solution.py:68
  319.8 2.8 copy-start.3
  319.8 47.6 %collective-permute-start.5 = (f32[4,16,64,64]{3,2,1,0:T(8,128)S(1)}, f32[4,16,64,64]{3,2,1,0:T(8,128)}, u32[]{:S(2)}, u32[]{:S(2)}) collective-permute-start(f32[4,16,64,64]{3,2,1,0:T(8,128)S(1)} %add.156), channel_id=1, source_target_pairs={{0,4},{1,5},{2,6},{3,7},{4,0},{5,1},{6,2},{7,3},{8,12},{9,13},{10,... | collective-permute-start | bytes 3145736 | tf_op jit(solution)/shard_map/ppermute | solution.py:68
  375.4 0.8 copy-start.1
  469.1 2.2 copy-start.10
  469.1 2.9 copy-start.12
Sparse Core Ops, SparseCore 0:
  144.1 74.6 all-gather.6
  376.4 71.8 all-gather.8
